TPU v7x, 512 devices: a whole 4x8x8 slice. The times are simulated.
512 devices in a mesh: blk: 64 (over x, z, y_lo), rep: 8 (over y_hi, core).
Axes of the slice: x: 4, y: 8 (y_hi: 4, y_lo: 2; y = y_hi * 2 + y_lo), z: 8, core: 2. Of those that a mesh axis runs over, the one named last changes fastest.
Arguments:
- grad_out: bfloat16 [65536, 256], P(('blk', 'rep')), may hold values from -6 to 6
- preact: bfloat16 [65536, 256], P(('blk', 'rep')), may hold values from -6 to 6
- aggregated: bfloat16 [65536, 256], P(('blk', 'rep')), may hold values from -6 to 6
- weight: bfloat16 [256, 256], replicated, may hold values from -0.375 to 0.375
- degree: int32 [65536], P(('blk', 'rep')), may hold values from 4 to 64
- neighbors: int32 [64, 8, 64, 4, 8, 128], P('blk', 'rep'), may hold values from 0 to 127
- tile_col: int32 [64, 8, 64, 4], P('blk', 'rep'), may hold values from 0 to 7, as said below
- tile_count: int32 [64, 8, 64], P('blk', 'rep'), may hold values from 0 to 4, as said below
Outputs:
- grad_features: bfloat16 [65536, 256], P(('blk', 'rep'))
- grad_weight: float32 [256, 256], replicated
Inputs may be any that keep to these rules, and one draw needn't show every extreme that they name: `tile_col`: the column tiles listed for one block, replica and source block are all different, also in slots at or past the count. `tile_count`: equal to 4 wherever the source block equals the block, and 0 wherever the source block is more than 2 blocks away from the block in both directions around the closed loop of 64 blocks.
All inputs are finite; a program needn't handle non-finite values.
Results may differ from a plain program's by a relative error of at most 0.0049.
Values may be sent and summed in bfloat16 or wider, within the bound.
No kernel may reach another device: no remote copies, remote signals or barrier semaphores. Data moves between devices by JAX's collectives and lax.ppermute only.
A program may use at most 64 MiB of HBM per device.

v0:
```python
import jax
import jax.numpy as jnp
from jax import lax
from jax.sharding import PartitionSpec as P

REACH = 2


def fetched_from(x, axis, offset):
    size = lax.axis_size(axis)
    return lax.ppermute(x, axis, [(i, (i - offset) % size) for i in range(size)])


def on_device(grad_out, preact, aggregated, weight, degree, neighbors, tile_col, tile_count):
    grad_pre = jnp.where(preact > 0, grad_out, jnp.zeros_like(grad_out))
    local_weight = lax.dot_general(
        aggregated, grad_pre, (((0,), (0,)), ((), ())), preferred_element_type=jnp.float32
    )
    raw_weight = lax.psum(local_weight, ("blk", "rep"))
    norm_value = jnp.sqrt(jnp.sum(raw_weight * raw_weight) + 1e-06)
    grad_weight = raw_weight * jnp.minimum(1.0, 128.0 / norm_value)
    inv_root = 1.0 / jnp.sqrt(degree.astype(jnp.float32))
    backward = lax.dot_general(
        grad_pre, weight, (((1,), (1,)), ((), ())), preferred_element_type=jnp.float32
    )
    scaled = (backward * inv_root[:, None]).astype(jnp.bfloat16)
    blocks = lax.axis_size("blk")
    replicas = lax.axis_size("rep")
    own_block = lax.axis_index("blk")
    offsets = list(range(-REACH, REACH + 1))
    rows = jnp.stack([scaled if d == 0 else fetched_from(scaled, "blk", d) for d in offsets])
    sources = (own_block + jnp.array(offsets, jnp.int32)) % blocks
    listed = jnp.take(neighbors[0, 0], sources, axis=0)
    column_ids = jnp.take(tile_col[0, 0], sources, axis=0)
    present = jnp.take(tile_count[0, 0], sources, axis=0)
    slots_total = listed.shape[1]
    tile_side = listed.shape[3]
    hidden = scaled.shape[1]
    positions = jnp.arange(tile_side, dtype=jnp.int32)
    slot_index = jnp.arange(slots_total, dtype=jnp.int32)
    counts = jnp.sum(
        (listed[:, :, :, :, None] == positions[None, None, None, None, :]).astype(jnp.int32), axis=2
    )
    chooser = jnp.logical_and(
        column_ids[:, :, None] == jnp.arange(replicas, dtype=jnp.int32)[None, None, :],
        (slot_index[None, :] < present[:, None])[:, :, None],
    ).astype(jnp.int32)
    merged = jnp.einsum("tsn,tsic->tinc", chooser, counts).astype(jnp.bfloat16)
    totals = jnp.einsum("tinc,tif->ncf", merged, rows, preferred_element_type=jnp.float32)
    owned = lax.psum_scatter(totals, "rep", scatter_dimension=0, tiled=True)
    grad_features = (owned[0] * inv_root[:, None]).astype(jnp.bfloat16)
    return (grad_features, grad_weight)


def solution(mesh):
    return jax.shard_map(
        on_device,
        mesh=mesh,
        in_specs=(
            P(("blk", "rep"), None),
            P(("blk", "rep"), None),
            P(("blk", "rep"), None),
            P(),
            P(("blk", "rep")),
            P("blk", "rep", None, None, None, None),
            P("blk", "rep", None, None),
            P("blk", "rep", None),
        ),
        out_specs=(P(("blk", "rep"), None), P()),
        check_vma=False,
    )
```

profile of v0, /device:TPU:23, one launch (start us, length us, event | category | flops | bytes accessed | tf_op | source)
XLA Modules:
  0.0 314.2 jit_solution(9490777069166894730)
XLA Ops:
  8.0 0.0 copy-start
  8.0 0.0 all-reduce.2.cloned.1.call-start
  8.1 0.7 convert_rsqrt_fusion
  8.8 1.2 fusion.2
  10.0 0.0 copy-start.2
  10.0 0.0 copy-start.1
  10.0 4.1 %collective-permute-start = (bf16[128,256]{1,0:T(8,128)(2,1)S(1)}, bf16[128,256]{1,0:T(8,128)(2,1)S(1)}, u32[]{:S(2)}, u32[]{:S(2)}) collective-permute-start(bf16[128,256]{1,0:T(8,128)(2,1)S(1)} %fusion.2), channel_id=1, source_target_pairs={{0,16},{8,24},{16,32},{24,40},{32,48},{40,56},{48,64},{56,72},{64,... | collective-permute-start | bytes 196616 | tf_op jit(solution)/shard_map/ppermute | solution.py:11
  14.1 3.2 %collective-permute-start.1 = (bf16[128,256]{1,0:T(8,128)(2,1)S(1)}, bf16[128,256]{1,0:T(8,128)(2,1)S(1)}, u32[]{:S(2)}, u32[]{:S(2)}) collective-permute-start(bf16[128,256]{1,0:T(8,128)(2,1)S(1)} %fusion.2), channel_id=1, source_target_pairs={{0,8},{8,16},{16,24},{24,32},{32,40},{40,48},{48,56},{56,64},{64,7... | collective-permute-start | bytes 196616 | tf_op jit(solution)/shard_map/ppermute | solution.py:11
  17.4 8.6 %collective-permute-start.2 = (bf16[128,256]{1,0:T(8,128)(2,1)S(1)}, bf16[128,256]{1,0:T(8,128)(2,1)S(1)}, u32[]{:S(2)}, u32[]{:S(2)}) collective-permute-start(bf16[128,256]{1,0:T(8,128)(2,1)S(1)} %fusion.2), channel_id=1, source_target_pairs={{0,504},{8,0},{16,8},{24,16},{32,24},{40,32},{48,40},{56,48},{64,5... | collective-permute-start | bytes 196616 | tf_op jit(solution)/shard_map/ppermute | solution.py:11
  25.9 3.4 %collective-permute-start.3 = (bf16[128,256]{1,0:T(8,128)(2,1)S(1)}, bf16[128,256]{1,0:T(8,128)(2,1)S(1)}, u32[]{:S(2)}, u32[]{:S(2)}) collective-permute-start(bf16[128,256]{1,0:T(8,128)(2,1)S(1)} %fusion.2), channel_id=1, source_target_pairs={{0,496},{8,504},{16,0},{24,8},{32,16},{40,24},{48,32},{56,40},{64,... | collective-permute-start | bytes 196616 | tf_op jit(solution)/shard_map/ppermute | solution.py:11
  29.3 1.8 convolution_bitcast_fusion.2
  31.1 0.0 all-reduce.2.cloned.1.call-update
  31.2 0.0 reduce-scatter.2.cloned.1.call-start
  31.2 0.7 compare_and_fusion
  31.9 0.0 copy-done
  31.9 0.6 gather_fusion
  32.5 0.1 broadcast_select_fusion
  32.5 4.2 %convert_reduce_fusion = s32[5,4,128,128]{3,2,1,0:T(8,128)S(1)} fusion(s32[5,4,8,128]{3,2,1,0:T(8,128)S(1)} %broadcast_select_fusion), kind=kLoop, calls=%fused_computation.3 | loop fusion | flops 7536640 | bytes 1392640 | tf_op jit(solution)/shard_map/reduce_sum | solution.py:41
  36.7 0.0 copy-done.2
  36.7 0.1 copy.15
  36.8 0.6 gather_fusion.1
  37.4 0.1 broadcast_select_fusion.1
  37.4 0.0 copy-done.1
  37.4 0.6 gather_fusion.2
  38.1 0.1 iota_compare_fusion.2
  38.2 2.8 convolution_bitcast_fusion
  41.0 0.0 collective-permute-done
  41.0 0.0 collective-permute-done.1
  41.1 0.0 collective-permute-done.2
  41.1 0.0 collective-permute-done.3
  41.1 1.6 convolution_bitcast_fusion.1
  42.7 0.0 reduce-scatter.2.cloned.1.call-update
  42.7 258.3 %all-reduce.2.cloned.1.call-done = f32[256,256]{0,1:T(8,128)} async-done(((f32[256,256]{0,1:T(8,128)}), f32[256,256]{0,1:T(8,128)}) %all-reduce.2.cloned.1.call-update) | async-done | bytes 262160 | tf_op jit(solution)/shard_map/psum | solution.py:19
  301.0 1.6 multiply_reduce_fusion
  303.3 1.0 broadcast_multiply_fusion
  304.3 0.8 copy.18
  305.2 0.0 reduce-scatter.2.cloned.1.call-done
  305.2 1.6 fusion.4
  (7 shorter events, 0.0 us)
Async XLA Ops:
  8.0 23.9 %copy-start = (s32[1,1,64,4,8,128]{5,4,3,2,1,0:T(8,128)S(1)}, s32[1,1,64,4,8,128]{5,4,3,2,1,0:T(8,128)}, u32[]{:S(2)}) copy-start(s32[1,1,64,4,8,128]{5,4,3,2,1,0:T(8,128)} %param.14) | copy-start | bytes 3145732
  8.0 293.0 %all-reduce.2.cloned.1.call-start = ((), (), s32[]{:S(2)}) async-start(), calls=%async_computation.2 | async-start | bytes 524288 | tf_op jit(solution)/shard_map/psum | solution.py:19
  10.0 26.7 %copy-start.2 = (s32[1,1,64,4]{2,3,1,0:T(4,128)S(1)}, s32[1,1,64,4]{2,3,1,0:T(4,128)}, u32[]{:S(2)}) copy-start(s32[1,1,64,4]{2,3,1,0:T(4,128)} %param.15) | copy-start | bytes 3076
  10.0 27.5 %copy-start.1 = (s32[1,1,64]{2,1,0:T(1,128)S(1)}, s32[1,1,64]{2,1,0:T(1,128)}, u32[]{:S(2)}) copy-start(s32[1,1,64]{2,1,0:T(1,128)} %param.16) | copy-start | bytes 772
  10.0 31.0 %collective-permute-start = (bf16[128,256]{1,0:T(8,128)(2,1)S(1)}, bf16[128,256]{1,0:T(8,128)(2,1)S(1)}, u32[]{:S(2)}, u32[]{:S(2)}) collective-permute-start(bf16[128,256]{1,0:T(8,128)(2,1)S(1)} %fusion.2), channel_id=1, source_target_pairs={{0,16},{8,24},{16,32},{24,40},{32,48},{40,56},{48,64},{56,72},{64,... | collective-permute-start | bytes 196616 | tf_op jit(solution)/shard_map/ppermute | solution.py:11
  14.1 26.9 %collective-permute-start.1 = (bf16[128,256]{1,0:T(8,128)(2,1)S(1)}, bf16[128,256]{1,0:T(8,128)(2,1)S(1)}, u32[]{:S(2)}, u32[]{:S(2)}) collective-permute-start(bf16[128,256]{1,0:T(8,128)(2,1)S(1)} %fusion.2), channel_id=1, source_target_pairs={{0,8},{8,16},{16,24},{24,32},{32,40},{40,48},{48,56},{56,64},{64,7... | collective-permute-start | bytes 196616 | tf_op jit(solution)/shard_map/ppermute | solution.py:11
  17.4 23.7 %collective-permute-start.2 = (bf16[128,256]{1,0:T(8,128)(2,1)S(1)}, bf16[128,256]{1,0:T(8,128)(2,1)S(1)}, u32[]{:S(2)}, u32[]{:S(2)}) collective-permute-start(bf16[128,256]{1,0:T(8,128)(2,1)S(1)} %fusion.2), channel_id=1, source_target_pairs={{0,504},{8,0},{16,8},{24,16},{32,24},{40,32},{48,40},{56,48},{64,5... | collective-permute-start | bytes 196616 | tf_op jit(solution)/shard_map/ppermute | solution.py:11
  25.9 15.1 %collective-permute-start.3 = (bf16[128,256]{1,0:T(8,128)(2,1)S(1)}, bf16[128,256]{1,0:T(8,128)(2,1)S(1)}, u32[]{:S(2)}, u32[]{:S(2)}) collective-permute-start(bf16[128,256]{1,0:T(8,128)(2,1)S(1)} %fusion.2), channel_id=1, source_target_pairs={{0,496},{8,504},{16,0},{24,8},{32,16},{40,24},{48,32},{56,40},{64,... | collective-permute-start | bytes 196616 | tf_op jit(solution)/shard_map/ppermute | solution.py:11
  31.2 274.0 %reduce-scatter.2.cloned.1.call-start = ((), (), s32[]{:S(2)}) async-start(), calls=%async_computation.1 | async-start | bytes 1179648 | tf_op jit(solution)/shard_map/reduce_scatter | solution.py:50
Sparse Core Ops, SparseCore 0:
  31.3 269.7 all-reduce.1
Sparse Core Ops, SparseCore 1:
  42.8 41.7 reduce-scatter.1
where the time goes:
time: 315 us; the launch traced here: 314 us
  waiting for transfers between devices  258 us (82%)
  starting transfers between devices  19.4 us (6%)
  between operations  16.4 us (5%)
  other arithmetic  10 us (3%)
  matrix products  7.4 us (2%)
    psum x1, waiting for transfers between devices, on_device(): raw_weight = lax.psum(local_weight, ('blk', 'rep'))  258 us
    ppermute x4, starting transfers between devices, fetched_from(): lax.ppermute(x, axis, [(i, (i - offset) % size) for i in range(size)])  19.3 us
  transfers between devices with their start and end apart: 6, of which 1 were waited for; matrix products, arithmetic and copies ran while one was open for 5% of the time, Pallas kernels for 0%

commit v1 on v0

--- a/solution.py
+++ b/solution.py
@@ -16,7 +16,9 @@
     local_weight = lax.dot_general(
         aggregated, grad_pre, (((0,), (0,)), ((), ())), preferred_element_type=jnp.float32
     )
-    raw_weight = lax.psum(local_weight, ("blk", "rep"))
+    raw_weight = local_weight
+    for over in ("blk", "rep"):
+        raw_weight = lax.psum(raw_weight, over)
     norm_value = jnp.sqrt(jnp.sum(raw_weight * raw_weight) + 1e-06)
     grad_weight = raw_weight * jnp.minimum(1.0, 128.0 / norm_value)
     inv_root = 1.0 / jnp.sqrt(degree.astype(jnp.float32))

time: 315 us -> 712 us (2.26)
  the two profiles are of different devices: /device:TPU:23 before, /device:TPU:17 now
where the time goes in v1:
time: 712 us
  waiting for transfers between devices  653 us (92%)
  starting transfers between devices  21.3 us (3%)
  between operations  14.6 us (2%)
  other arithmetic  11.1 us (2%)
  matrix products  8.66 us (1%)
    psum x2, waiting for transfers between devices, on_device(): raw_weight = lax.psum(raw_weight, over)  613 us
    reduce_scatter x1, waiting for transfers between devices, on_device(): owned = lax.psum_scatter(totals, 'rep', scatter_dimension=0, tiled=True)  40.1 us
    ppermute x4, starting transfers between devices, fetched_from(): lax.ppermute(x, axis, [(i, (i - offset) % size) for i in range(size)])  21.2 us
  transfers between devices with their start and end apart: 7, of which 3 were waited for; matrix products, arithmetic and copies ran while one was open for 3% of the time, Pallas kernels for 0%

profile of v1, /device:TPU:17, one launch (start us, length us, event | category | flops | bytes accessed | tf_op | source)
XLA Modules:
  0.0 711.6 jit_solution(11009445770341718081)
XLA Ops:
  7.2 0.0 copy-start
  7.2 0.0 all-reduce.3.cloned.1.call-start
  7.2 0.7 convert_rsqrt_fusion
  8.0 1.2 fusion.2
  9.1 0.0 copy-start.2
  9.2 0.0 copy-start.1
  9.2 4.1 collective-permute-start
  13.3 3.2 collective-permute-start.1
  16.5 10.5 %collective-permute-start.2 = (bf16[128,256]{1,0:T(8,128)(2,1)S(1)}, bf16[128,256]{1,0:T(8,128)(2,1)S(1)}, u32[]{:S(2)}, u32[]{:S(2)}) collective-permute-start(bf16[128,256]{1,0:T(8,128)(2,1)S(1)} %fusion.2), channel_id=1, source_target_pairs={{0,504},{8,0},{16,8},{24,16},{32,24},{40,32},{48,40},{56,48},{64,5... | collective-permute-start | bytes 196616 | tf_op jit(solution)/shard_map/ppermute | solution.py:11
  27.0 3.4 collective-permute-start.3
  30.4 1.8 convolution_bitcast_fusion.2
  32.2 0.0 all-reduce.3.cloned.1.call-update
  32.2 0.0 all-reduce.5.cloned.1.call-start
  32.3 0.7 compare_and_fusion
  33.0 0.0 copy-done
  33.0 0.6 gather_fusion
  33.6 0.1 broadcast_select_fusion
  33.6 5.2 convert_reduce_fusion
  38.8 0.0 copy-done.2
  38.9 0.1 copy.15
  38.9 0.6 gather_fusion.1
  39.5 0.1 broadcast_select_fusion.1
  39.6 0.0 copy-done.1
  39.6 0.6 gather_fusion.2
  40.2 0.1 iota_compare_fusion.2
  40.3 4.1 convolution_bitcast_fusion
  44.4 0.0 collective-permute-done
  44.4 0.0 collective-permute-done.1
  44.5 0.0 collective-permute-done.2
  44.5 510.8 %all-reduce.3.cloned.1.call-done = f32[256,256]{0,1:T(8,128)} async-done(((f32[256,256]{0,1:T(8,128)}), f32[256,256]{0,1:T(8,128)}) %all-reduce.3.cloned.1.call-update) | async-done | bytes 262160 | tf_op jit(solution)/shard_map/psum | solution.py:21
  555.3 0.0 all-reduce.5.cloned.1.call-update
  555.3 0.0 reduce-scatter.2.cloned.1.call-start
  555.4 0.0 collective-permute-done.3
  555.4 1.6 convolution_bitcast_fusion.1
  557.0 0.0 reduce-scatter.2.cloned.1.call-update
  557.0 102.3 %all-reduce.5.cloned.1.call-done = f32[256,256]{0,1:T(8,128)} async-done(((f32[256,256]{0,1:T(8,128)}), f32[256,256]{0,1:T(8,128)}) %all-reduce.5.cloned.1.call-update) | async-done | bytes 262160 | tf_op jit(solution)/shard_map/psum | solution.py:21
  659.3 1.6 multiply_reduce_fusion
  661.6 1.0 broadcast_multiply_fusion
  662.5 0.8 copy.18
  663.4 40.1 %reduce-scatter.2.cloned.1.call-done = f32[1,128,256]{2,1,0:T(8,128)} async-done(((f32[8,128,256]{2,1,0:T(8,128)}), f32[1,128,256]{2,1,0:T(8,128)}) %reduce-scatter.2.cloned.1.call-update) | async-done | bytes 131088 | tf_op jit(solution)/shard_map/reduce_scatter | solution.py:52
  703.5 1.6 fusion.4
  (7 shorter events, 0.0 us)
Async XLA Ops:
  7.2 25.8 %copy-start = (s32[1,1,64,4,8,128]{5,4,3,2,1,0:T(8,128)S(1)}, s32[1,1,64,4,8,128]{5,4,3,2,1,0:T(8,128)}, u32[]{:S(2)}) copy-start(s32[1,1,64,4,8,128]{5,4,3,2,1,0:T(8,128)} %param.14) | copy-start | bytes 3145732
  7.2 548.1 %all-reduce.3.cloned.1.call-start = ((), (), s32[]{:S(2)}) async-start(), calls=%async_computation.2 | async-start | bytes 524288 | tf_op jit(solution)/shard_map/psum | solution.py:21
  9.1 29.7 %copy-start.2 = (s32[1,1,64,4]{2,3,1,0:T(4,128)S(1)}, s32[1,1,64,4]{2,3,1,0:T(4,128)}, u32[]{:S(2)}) copy-start(s32[1,1,64,4]{2,3,1,0:T(4,128)} %param.15) | copy-start | bytes 3076
  9.2 30.4 %copy-start.1 = (s32[1,1,64]{2,1,0:T(1,128)S(1)}, s32[1,1,64]{2,1,0:T(1,128)}, u32[]{:S(2)}) copy-start(s32[1,1,64]{2,1,0:T(1,128)} %param.16) | copy-start | bytes 772
  9.2 35.2 %collective-permute-start = (bf16[128,256]{1,0:T(8,128)(2,1)S(1)}, bf16[128,256]{1,0:T(8,128)(2,1)S(1)}, u32[]{:S(2)}, u32[]{:S(2)}) collective-permute-start(bf16[128,256]{1,0:T(8,128)(2,1)S(1)} %fusion.2), channel_id=1, source_target_pairs={{0,16},{8,24},{16,32},{24,40},{32,48},{40,56},{48,64},{56,72},{64,... | collective-permute-start | bytes 196616 | tf_op jit(solution)/shard_map/ppermute | solution.py:11
  13.3 31.1 %collective-permute-start.1 = (bf16[128,256]{1,0:T(8,128)(2,1)S(1)}, bf16[128,256]{1,0:T(8,128)(2,1)S(1)}, u32[]{:S(2)}, u32[]{:S(2)}) collective-permute-start(bf16[128,256]{1,0:T(8,128)(2,1)S(1)} %fusion.2), channel_id=1, source_target_pairs={{0,8},{8,16},{16,24},{24,32},{32,40},{40,48},{48,56},{56,64},{64,7... | collective-permute-start | bytes 196616 | tf_op jit(solution)/shard_map/ppermute | solution.py:11
  16.5 27.9 %collective-permute-start.2 = (bf16[128,256]{1,0:T(8,128)(2,1)S(1)}, bf16[128,256]{1,0:T(8,128)(2,1)S(1)}, u32[]{:S(2)}, u32[]{:S(2)}) collective-permute-start(bf16[128,256]{1,0:T(8,128)(2,1)S(1)} %fusion.2), channel_id=1, source_target_pairs={{0,504},{8,0},{16,8},{24,16},{32,24},{40,32},{48,40},{56,48},{64,5... | collective-permute-start | bytes 196616 | tf_op jit(solution)/shard_map/ppermute | solution.py:11
  27.0 528.3 %collective-permute-start.3 = (bf16[128,256]{1,0:T(8,128)(2,1)S(1)}, bf16[128,256]{1,0:T(8,128)(2,1)S(1)}, u32[]{:S(2)}, u32[]{:S(2)}) collective-permute-start(bf16[128,256]{1,0:T(8,128)(2,1)S(1)} %fusion.2), channel_id=1, source_target_pairs={{0,496},{8,504},{16,0},{24,8},{32,16},{40,24},{48,32},{56,40},{64,... | collective-permute-start | bytes 196616 | tf_op jit(solution)/shard_map/ppermute | solution.py:11
  32.2 627.0 %all-reduce.5.cloned.1.call-start = ((), (), s32[]{:S(2)}) async-start(), calls=%async_computation.3 | async-start | bytes 524288 | tf_op jit(solution)/shard_map/psum | solution.py:21
  555.3 148.1 %reduce-scatter.2.cloned.1.call-start = ((), (), s32[]{:S(2)}) async-start(), calls=%async_computation.1 | async-start | bytes 1179648 | tf_op jit(solution)/shard_map/reduce_scatter | solution.py:52
Sparse Core Ops, SparseCore 0:
  32.4 522.8 all-reduce.2
  558.5 100.7 all-reduce.4
  662.1 41.3 reduce-scatter.1
